TPU v7x, 32 devices: a whole 2x2x4 slice. The times are simulated.
32 devices in a mesh: dp: 16 (over z, y, core), ctx: 2 (over x).
Axes of the slice: x: 2, y: 2, z: 4, core: 2. Of those that a mesh axis runs over, the one named last changes fastest.
Arguments:
- tokens: bfloat16 [16, 2, 384, 8192], P('dp', 'ctx'), may hold values from -6 to 6
- lengths: int32 [16, 2], P('dp'), may hold values from 96 to 384, as said below
- norm_gain: float32 [8192], replicated, may hold values from 0.5 to 1.5
- w_in: bfloat16 [8192, 1536], P('dp'), may hold values from -0.0625 to 0.0625
- short_filter: float32 [3, 1536], replicated, may hold values from -3.5 to 3.5
- decay_rate: float32 [16, 512], replicated, may hold values from 5e-05 to 0.03
- residue: float32 [16, 512], replicated, may hold values from -0.12 to 0.12
- skip_gain: float32 [512], replicated, may hold values from -6 to 6
- w_out: bfloat16 [512, 8192], P(None, 'dp'), may hold values from -0.25 to 0.25
- steer_table: float32 [50, 2, 8192], replicated, may hold values from -3 to 3
- steer_layer: int32 [16], P('dp'), may hold values from 0 to 49
- steer_slab: int32 [16], P('dp'), may hold values from 0 to 7
Outputs:
- result: bfloat16 [16, 2, 384, 8192], P('dp', 'ctx')
Inputs may be any that keep to these rules, and one draw needn't show every extreme that they name: `lengths`: each group holds 96 to 384 live tokens; in every sequence one group holds exactly 384.
All inputs are finite; a program needn't handle non-finite values.
Results may differ from a plain program's by a relative error of at most 0.004.
The roundings to bfloat16 on the way count: a program that leaves them out, or rounds other values in their place, can miss the bound.
Values may be sent and summed in bfloat16 or wider, within the bound.
No kernel may reach another device: no remote copies, remote signals or barrier semaphores. Data moves between devices by JAX's collectives and lax.ppermute only.
A program may use at most 192 MiB of HBM per device.

v0:
```python
import jax
import jax.numpy as jnp
from jax import lax
from jax.sharding import PartitionSpec as P

STEER_W = 1024
BLOCK = 32


def from_behind(value, axis, steps):
    count = lax.axis_size(axis)
    first, last = (max(0, -steps), min(count, count - steps))
    return lax.ppermute(value, axis, [(source, source + steps) for source in range(first, last)])


def normalize(rows_in, gain):
    values = rows_in.astype(jnp.float32)
    scale = lax.rsqrt(jnp.mean(values * values, axis=1, keepdims=True) + 1e-06)
    return (values * scale * gain[None, :]).astype(jnp.bfloat16)


def filter_tables(decay_rate, residue, block):
    lags = jnp.arange(block)
    lags_float = lags.astype(jnp.float32)
    taps = jnp.sum(residue[None] * jnp.exp(-decay_rate[None] * lags_float[:, None, None]), axis=1)
    diff = lags[:, None] - lags[None, :]
    toeplitz = jnp.where((diff >= 0)[:, :, None], taps[jnp.clip(diff, 0, block - 1)], 0.0)
    toeplitz = jnp.transpose(toeplitz, (1, 0, 2))
    lead = residue[:, None] * jnp.exp(-decay_rate[:, None] * (lags_float + 1.0)[None, :, None])
    close = jnp.exp(-decay_rate[None] * (block - 1 - lags_float)[:, None, None])
    return (toeplitz, lead, close)


def block_states(drive, decay_rate, close, block):
    cap, width = drive.shape
    count = cap // block
    pieces = drive.reshape(count, block, width)
    ends = jnp.sum(close[None] * pieces[:, :, None, :], axis=1)
    steps = jnp.arange(count)
    gap = (steps[:, None] - steps[None, :]).astype(jnp.float32)
    powers = jnp.where(
        (gap >= 0)[:, :, None, None],
        jnp.exp(-decay_rate[None, None] * (block * jnp.maximum(gap, 0.0))[:, :, None, None]),
        0.0,
    )
    return jnp.sum(powers * ends[None], axis=1)


def block_outputs(drive, states, incoming, decay_rate, toeplitz, lead, block):
    cap, width = drive.shape
    count = cap // block
    pieces = drive.reshape(count, block, width)
    inside = jnp.sum(toeplitz[None] * pieces[:, :, None, :], axis=1)
    starts = (jnp.arange(count) * block).astype(jnp.float32)
    carried = incoming[None] * jnp.exp(-decay_rate[None] * starts[:, None, None])
    before = jnp.concatenate([jnp.zeros_like(states[:1]), states[:-1]], axis=0) + carried
    earlier = jnp.sum(lead[None] * before[:, :, None, :], axis=1)
    return (inside + earlier).reshape(cap, width)


def per_device(
    tokens,
    lengths,
    norm_gain,
    w_in,
    short_filter,
    decay_rate,
    residue,
    skip_gain,
    w_out,
    steer_table,
    steer_layer,
    steer_slab,
):
    cap = tokens.shape[2]
    width = tokens.shape[3]
    slab = residue.shape[1]
    groups = lax.axis_size("ctx")
    rows_in = tokens.reshape(cap, width)
    normed = normalize(rows_in, norm_gain)
    position = lax.axis_index("ctx")
    group_lens = lengths.reshape(-1)
    own_len = lax.dynamic_index_in_dim(group_lens, position, 0, keepdims=False)
    live = jnp.arange(cap) < own_len
    own_tail = lax.dynamic_slice_in_dim(normed, own_len - 2, 2, 0)
    tail_normed = from_behind(own_tail, "ctx", 1)
    block = BLOCK if cap % BLOCK == 0 else cap
    toeplitz, lead, close = filter_tables(decay_rate, residue, block)
    lens_f = group_lens.astype(jnp.float32)
    cumlen = jnp.cumsum(lens_f)
    rescale = jnp.exp(decay_rate * (cap - own_len).astype(jnp.float32))
    piece = jnp.concatenate([w_in, w_out.T], axis=1)
    gathered = lax.all_gather(piece, "dp", axis=0, tiled=True)
    w_in_all = gathered[:, : 3 * slab]
    w_out_t = gathered[:, 3 * slab :]
    rows_ext = jnp.concatenate([tail_normed, normed], axis=0)
    extended = jnp.dot(rows_ext, w_in_all, preferred_element_type=jnp.float32)
    extended = lax.reduce_precision(extended, exponent_bits=8, mantissa_bits=7)
    feat = (
        short_filter[0] * extended[2:]
        + short_filter[1] * extended[1:-1]
        + short_filter[2] * extended[:-2]
    )
    gate = feat[:, :slab]
    drive = jnp.where(live[:, None], feat[:, slab : 2 * slab] * feat[:, 2 * slab :], 0.0)
    states = block_states(drive, decay_rate, close, block)
    ending = states[-1] * rescale
    incoming = jnp.zeros_like(ending)
    for k in range(1, groups):
        got = from_behind(ending, "ctx", k)
        source = position - k
        between = lax.dynamic_index_in_dim(
            cumlen, jnp.maximum(position - 1, 0), 0, keepdims=False
        ) - lax.dynamic_index_in_dim(cumlen, jnp.maximum(source, 0), 0, keepdims=False)
        weight = jnp.where(source >= 0, jnp.exp(-decay_rate * between), 0.0)
        incoming = incoming + weight * got
    local = block_outputs(drive, states, incoming, decay_rate, toeplitz, lead, block)
    filtered = local + skip_gain[None, :] * drive
    gated = jnp.where(live[:, None], gate * filtered, 0.0).astype(jnp.bfloat16)
    mixed = lax.dot_general(
        gated, w_out_t, (((1,), (1,)), ((), ())), preferred_element_type=jnp.float32
    )
    rows2 = lax.dynamic_index_in_dim(steer_table, steer_layer[0], 0, keepdims=False)
    shift_vec = rows2[0] - rows2[1]
    columns = jnp.arange(width) // STEER_W
    steer = jnp.where(columns == steer_slab[0], 2.0 * shift_vec, 0.0)
    summed = rows_in.astype(jnp.float32) + mixed + steer[None, :]
    summed = jnp.where(live[:, None], summed, 0.0)
    return summed.astype(jnp.bfloat16).reshape(tokens.shape)


def solution(mesh):
    placed = (
        P("dp", "ctx", None, None),
        P("dp", None),
        P(),
        P("dp", None),
        P(),
        P(),
        P(),
        P(),
        P(None, "dp"),
        P(),
        P("dp"),
        P("dp"),
    )
    return jax.shard_map(
        per_device,
        mesh=mesh,
        in_specs=placed,
        out_specs=P("dp", "ctx", None, None),
        check_vma=False,
    )
```

profile of v0, /device:TPU:0, one launch (start us, length us, event | category | flops | bytes accessed | tf_op | source)
XLA Modules:
  0.0 229.9 jit_solution(1049465095491891067)
XLA Ops:
  6.5 1.3 copy.17
  7.8 3.0 %pad_maximum_fusion = bf16[512,2048]{1,0:T(8,128)(2,1)} fusion(bf16[512,512]{1,0:T(8,128)(2,1)S(1)} %copy.17, bf16[512,1536]{1,0:T(8,128)(2,1)} %param.15), kind=kLoop, calls=%fused_computation.27 | loop fusion | flops 4194304 | bytes 4194304 | tf_op jit(solution)/shard_map/concatenate | solution.py:92
  10.9 0.7 constant_dynamic-slice_fusion.2
  12.9 4.1 %fusion.2 = f32[384]{0:T(512)S(1)} fusion(bf16[1,1,384,8192]{3,2,1,0:T(8,128)(2,1)} %param.12), kind=kLoop, calls=%fused_computation.7 | loop fusion | flops 9436800 | bytes 6292992 | tf_op jit(solution)/shard_map/reduce_sum | solution.py:18
  17.1 4.7 %fusion.4 = bf16[384,8192]{1,0:T(8,128)(2,1)S(1)} fusion(bf16[1,1,384,8192]{3,2,1,0:T(8,128)(2,1)} %param.12, f32[8192]{0:T(1024)S(1)} %copy-done.5, f32[384]{0:T(512)S(1)} %add_rsqrt_fusion), kind=kLoop, calls=%fused_computation.9 | loop fusion | flops 12582912 | bytes 12617216 | tf_op jit(solution)/shard_map/convert_element_type | solution.py:19
  21.8 2.7 %copy-done.1 = bf16[384,8192]{1,0:T(8,128)(2,1)} copy-done((bf16[384,8192]{1,0:T(8,128)(2,1)}, bf16[384,8192]{1,0:T(8,128)(2,1)S(1)}, u32[]{:S(2)}) %copy-start.1) | copy-done | bytes 6291480
  24.6 5.7 %collective-permute-start = (bf16[2,8192]{1,0:T(2,128)(2,1)S(1)}, bf16[2,8192]{1,0:T(2,128)(2,1)S(1)}, u32[]{:S(2)}, u32[]{:S(2)}) collective-permute-start(bf16[2,8192]{1,0:T(2,128)(2,1)S(1)} %constant_dynamic-slice_fusion.1), channel_id=1, source_target_pairs={{0,1},{2,3},{4,5},{6,7},{8,9},{10,11},{12,13},{14,15},{16,17},{18,... | collective-permute-start | bytes 98312 | tf_op jit(solution)/shard_map/ppermute | solution.py:13
  31.7 1.4 multiply_exponential_fusion
  33.2 4.8 %gather_fusion = f32[1024,512]{1,0:T(8,128)} fusion(f32[32,512]{1,0:T(8,128)S(1)} %get-tuple-element.9, s32[1024]{0:T(1024)S(1)} %broadcast_clamp_fusion), kind=kCustom, calls=%fused_computation | custom fusion | bytes 4198400 | tf_op jit(solution)/shard_map/gather | solution.py:27
  38.0 1.3 iota_compare_fusion
  39.3 0.6 convert_compare_fusion
  39.9 0.6 maximum_multiply_fusion
  40.5 0.6 slice_reduce_fusion.2
  41.2 1.0 fusion.26
  42.1 0.2 exponential_multiply_fusion
  42.4 1.8 broadcast_select_fusion
  44.2 0.6 multiply_convert_fusion
  45.5 2.6 %copy.18 = f32[32,32,512]{2,1,0:T(8,128)} copy(f32[32,32,512]{2,0,1:T(8,128)S(1)} %broadcast_select_fusion) | data formatting | bytes 4194304 | tf_op jit(solution)/shard_map/jit(_where)/select_n | solution.py:27
  48.1 0.2 reduce-window.4
  48.2 0.7 fusion.31
  48.9 0.6 copy-done.12
  49.5 132.3 %all-gather.2.cloned.1.call-done = bf16[8192,2048]{1,0:T(8,128)(2,1)} async-done(((bf16[512,2048]{1,0:T(8,128)(2,1)}), bf16[8192,2048]{1,0:T(8,128)(2,1)}) %all-gather.2.cloned.1.call-update) | async-done | bytes 33554448 | tf_op jit(solution)/shard_map/all_gather | solution.py:93
  181.8 16.7 %fusion.13 = f32[386,1536]{1,0:T(8,128)S(1)} fusion(bf16[8192,2048]{1,0:T(8,128)(2,1)} %all-gather.2.cloned.1.call-done, bf16[384,8192]{1,0:T(8,128)(2,1)} %copy-done.1, bf16[2,8192]{1,0:T(2,128)(2,1)} %copy-done.12), kind=kOutput, calls=%fused_computation.21 | convolution fusion | flops 9727249408 | bytes 33861632 | tf_op jit(solution)/shard_map/dot_general | solution.py:97
  198.6 1.6 fusion.18
  200.3 1.1 multiply_reduce_fusion.2
  201.4 1.3 multiply_reduce_fusion.3
  202.8 3.6 %collective-permute-start.1 = (f32[16,512]{1,0:T(8,128)S(1)}, f32[16,512]{1,0:T(8,128)S(1)}, u32[]{:S(2)}, u32[]{:S(2)}) collective-permute-start(f32[16,512]{1,0:T(8,128)S(1)} %fusion.27), channel_id=1, source_target_pairs={{0,1},{2,3},{4,5},{6,7},{8,9},{10,11},{12,13},{14,15},{16,17},{18,... | collective-permute-start | bytes 98312 | tf_op jit(solution)/shard_map/ppermute | solution.py:13
  206.4 2.4 %multiply_reduce_fusion = f32[12,32,512]{2,1,0:T(8,128)S(1)} fusion(f32[12,32,512]{2,1,0:T(8,128)S(1)} %bitcast.36, f32[32,32,512]{2,1,0:T(8,128)S(1)} %copy-done), kind=kLoop, calls=%fused_computation.3 | loop fusion | flops 12386304 | bytes 3670016 | tf_op jit(solution)/shard_map/reduce_sum | solution.py:53
  208.9 0.7 select_multiply_fusion
  209.8 1.0 multiply_reduce_fusion.1
  210.9 0.2 fusion.22
  211.2 11.9 %fusion.8 = bf16[1,1,384,8192]{3,2,1,0:T(8,128)(2,1)} fusion(bf16[384,512]{1,0:T(8,128)(2,1)S(1)} %fusion.22, bf16[8192,2048]{1,0:T(8,128)(2,1)} %all-gather.2.cloned.1.call-done, bf16[1,1,384,8192]{3,2,1,0:T(8,128)(2,1)} %param.12, f32[8192]{0:T(1024)S(1)} %fusion.29, pred[384]{0:T(512)(128)(4,1)S(1)} %copy-done.9), kind=kOutput, calls=%fused_computation.15 | convolution fusion | flops 3236954112 | bytes 21397888 | tf_op jit(solution)/shard_map/dot_general | solution.py:120
  (47 shorter events, 0.7 us)
Async XLA Ops:
  6.5 4.4 %copy-start.13 = (s32[1,2]{1,0:T(1,128)S(1)}, s32[1,2]{1,0:T(1,128)}, u32[]{:S(2)}) copy-start(s32[1,2]{1,0:T(1,128)} %param.13) | copy-start | bytes 28
  6.5 175.3 %all-gather.2.cloned.1.call-start = ((), (), s32[]{:S(2)}) async-start(), calls=%async_computation | async-start | bytes 35651584 | tf_op jit(solution)/shard_map/all_gather | solution.py:93
  7.8 9.3 %copy-start.5 = (f32[8192]{0:T(1024)S(1)}, f32[8192]{0:T(1024)}, u32[]{:S(2)}) copy-start(f32[8192]{0:T(1024)} %param.14) | copy-start | bytes 98308
  17.1 13.2 %copy-start.3 = (f32[16,512]{1,0:T(8,128)S(1)}, f32[16,512]{1,0:T(8,128)}, u32[]{:S(2)}) copy-start(f32[16,512]{1,0:T(8,128)} %param.17) | copy-start | bytes 98308
  17.1 14.6 %copy-start.4 = (f32[16,512]{1,0:T(8,128)S(1)}, f32[16,512]{1,0:T(8,128)}, u32[]{:S(2)}) copy-start(f32[16,512]{1,0:T(8,128)} %param.18) | copy-start | bytes 98308
  21.8 2.7 %copy-start.1 = (bf16[384,8192]{1,0:T(8,128)(2,1)}, bf16[384,8192]{1,0:T(8,128)(2,1)S(1)}, u32[]{:S(2)}) copy-start(bf16[384,8192]{1,0:T(8,128)(2,1)S(1)} %fusion.4) | copy-start | bytes 18874372
  24.6 24.3 %collective-permute-start = (bf16[2,8192]{1,0:T(2,128)(2,1)S(1)}, bf16[2,8192]{1,0:T(2,128)(2,1)S(1)}, u32[]{:S(2)}, u32[]{:S(2)}) collective-permute-start(bf16[2,8192]{1,0:T(2,128)(2,1)S(1)} %constant_dynamic-slice_fusion.1), channel_id=1, source_target_pairs={{0,1},{2,3},{4,5},{6,7},{8,9},{10,11},{12,13},{14,15},{16,17},{18,... | collective-permute-start | bytes 98312 | tf_op jit(solution)/shard_map/ppermute | solution.py:13
  33.2 7.3 %copy-start.6 = (f32[3,1536]{1,0:T(4,128)S(1)}, f32[3,1536]{1,0:T(4,128)}, u32[]{:S(2)}) copy-start(f32[3,1536]{1,0:T(4,128)} %param.16) | copy-start | bytes 55300
  48.9 0.6 copy-start.12
  198.5 1.6 copy-start.9
  198.6 1.8 copy-start.2
  198.6 2.9 %copy-start.7 = (f32[12,12]{1,0:T(8,128)S(1)}, f32[12,12]{1,0:T(8,128)}, u32[]{:S(2)}) copy-start(f32[12,12]{1,0:T(8,128)} %maximum_multiply_fusion) | copy-start | bytes 1732
  198.6 2.9 %copy-start.10 = (pred[12,12]{1,0:T(8,128)(4,1)S(1)}, pred[12,12]{1,0:T(8,128)(4,1)}, u32[]{:S(2)}) copy-start(pred[12,12]{1,0:T(8,128)(4,1)} %convert_compare_fusion) | copy-start | bytes 436
  198.6 7.8 %copy-start = (f32[32,32,512]{2,1,0:T(8,128)S(1)}, f32[32,32,512]{2,1,0:T(8,128)}, u32[]{:S(2)}) copy-start(f32[32,32,512]{2,1,0:T(8,128)} %copy.18) | copy-start | bytes 6291460
  200.2 9.4 %copy-start.11 = (f32[12]{0:T(128)S(1)}, f32[12]{0:T(128)}, u32[]{:S(2)}) copy-start(f32[12]{0:T(128)} %multiply_convert_fusion) | copy-start | bytes 148
  201.4 9.5 %copy-start.8 = (f32[512]{0:T(512)S(1)}, f32[512]{0:T(512)}, u32[]{:S(2)}) copy-start(f32[512]{0:T(512)} %param.19) | copy-start | bytes 6148
  202.8 6.1 %collective-permute-start.1 = (f32[16,512]{1,0:T(8,128)S(1)}, f32[16,512]{1,0:T(8,128)S(1)}, u32[]{:S(2)}, u32[]{:S(2)}) collective-permute-start(f32[16,512]{1,0:T(8,128)S(1)} %fusion.27), channel_id=1, source_target_pairs={{0,1},{2,3},{4,5},{6,7},{8,9},{10,11},{12,13},{14,15},{16,17},{18,... | collective-permute-start | bytes 98312 | tf_op jit(solution)/shard_map/ppermute | solution.py:13
Sparse Core Ops, SparseCore 0:
  11.0 170.7 all-gather.1
where the time goes:
time: 230 us
  waiting for transfers between devices  132 us (57%)
  other arithmetic  29.1 us (13%)
  matrix products  28.7 us (12%)
  between operations  17.2 us (7%)
  local copies, waits for them, and re-layouts  13.5 us (6%)
  starting transfers between devices  9.25 us (4%)
    all_gather x1, waiting for transfers between devices, per_device(): gathered = lax.all_gather(piece, 'dp', axis=0, tiled=True)  132 us
    dot_general x1, matrix products, per_device(): extended = jnp.dot(rows_ext, w_in_all, preferred_element_type=jnp.float32)  16.7 us
    dot_general x1, matrix products, per_device(): lax.dot_general(gated, w_out_t, (((1,), (1,)), ((), ())), preferred_eleme...  11.9 us
    ppermute x2, starting transfers between devices, from_behind(): lax.ppermute(value, axis, [(source, source + steps) for source in range(f...  9.25 us
    gather x1, local copies, waits for them, and re-layouts, filter_tables(): taps[jnp.clip(diff, 0, block - 1)]  4.84 us
    convert_element_type x1, other arithmetic, normalize(): return (values * scale * gain[None, :]).astype(jnp.bfloat16)  4.73 us
  transfers between devices with their start and end apart: 3, of which 1 were waited for; matrix products, arithmetic and copies ran while one was open for 12% of the time, Pallas kernels for 0%

commit v1 on v0

--- a/solution.py
+++ b/solution.py
@@ -90,7 +90,12 @@
     cumlen = jnp.cumsum(lens_f)
     rescale = jnp.exp(decay_rate * (cap - own_len).astype(jnp.float32))
     piece = jnp.concatenate([w_in, w_out.T], axis=1)
-    gathered = lax.all_gather(piece, "dp", axis=0, tiled=True)
+    ring = [piece]
+    for hop in range(15):
+        ring.append(lax.ppermute(ring[-1], "dp", [(dev, (dev + 1) % 16) for dev in range(16)]))
+    gathered = jnp.roll(
+        jnp.concatenate(ring[::-1], axis=0), (lax.axis_index("dp") + 1) * ring[0].shape[0], axis=0
+    )
     w_in_all = gathered[:, : 3 * slab]
     w_out_t = gathered[:, 3 * slab :]
     rows_ext = jnp.concatenate([tail_normed, normed], axis=0)

time: 230 us -> 546 us (2.37)
  waiting for transfers between devices: 132 us -> 392 us
  local copies, waits for them, and re-layouts: 13.5 us -> 84.4 us
  between operations: 17.2 us -> 3.76 us
    ppermute x0 -> x15, waiting for transfers between devices: none -> 392 us  [per_device(): lax.ppermute(ring[-1], 'dp', [(dev, (dev + 1) % 16) for dev in range(16)])]
    all_gather x1 -> x0, waiting for transfers between devices: 132 us -> none  [per_device(): gathered = lax.all_gather(piece, 'dp', axis=0, tiled=True)]
    unnamed x28 -> x92, local copies, waits for them, and re-layouts: 3.36 us -> 74.2 us
  transfers between devices with their start and end apart: 3 -> 17, of which waited for: 1 -> 15; matrix products, arithmetic and copies ran while one was open for 12% -> 17% of each run, Pallas kernels for 0% -> 0%
where the time goes in v1:
time: 546 us
  waiting for transfers between devices  392 us (72%)
  local copies, waits for them, and re-layouts  84.4 us (15%)
  other arithmetic  29.9 us (5%)
  matrix products  27.7 us (5%)
  starting transfers between devices  8.21 us (2%)
    ppermute x15, waiting for transfers between devices, per_device(): lax.ppermute(ring[-1], 'dp', [(dev, (dev + 1) % 16) for dev in range(16)])  392 us
    unnamed x92, local copies, waits for them, and re-layouts  74.2 us
    dot_general x1, matrix products, per_device(): extended = jnp.dot(rows_ext, w_in_all, preferred_element_type=jnp.float32)  15.7 us
    dot_general x1, matrix products, per_device(): lax.dot_general(gated, w_out_t, (((1,), (1,)), ((), ())), preferred_eleme...  12 us
  transfers between devices with their start and end apart: 17, of which 15 were waited for; matrix products, arithmetic and copies ran while one was open for 17% of the time, Pallas kernels for 0%

profile of v1, /device:TPU:0, one launch (start us, length us, event | category | flops | bytes accessed | tf_op | source)
XLA Modules:
  0.0 545.7 jit_solution(3431432635606216492)
XLA Ops:
  3.4 28.7 %collective-permute-done.1 = bf16[512,2048]{1,0:T(8,128)(2,1)S(1)} collective-permute-done((bf16[512,2048]{1,0:T(8,128)(2,1)S(1)}, bf16[512,2048]{1,0:T(8,128)(2,1)S(1)}, u32[]{:S(2)}, u32[]{:S(2)}) %collective-permute-start.1) | collective-permute-done | bytes 2097184 | tf_op jit(solution)/shard_map/ppermute | solution.py:95
  33.5 28.2 %collective-permute-done.2 = bf16[512,2048]{1,0:T(8,128)(2,1)S(1)} collective-permute-done((bf16[512,2048]{1,0:T(8,128)(2,1)S(1)}, bf16[512,2048]{1,0:T(8,128)(2,1)S(1)}, u32[]{:S(2)}, u32[]{:S(2)}) %collective-permute-start.2) | collective-permute-done | bytes 2097184 | tf_op jit(solution)/shard_map/ppermute | solution.py:95
  63.0 28.2 %collective-permute-done.3 = bf16[512,2048]{1,0:T(8,128)(2,1)S(1)} collective-permute-done((bf16[512,2048]{1,0:T(8,128)(2,1)S(1)}, bf16[512,2048]{1,0:T(8,128)(2,1)S(1)}, u32[]{:S(2)}, u32[]{:S(2)}) %collective-permute-start.3) | collective-permute-done | bytes 2097184 | tf_op jit(solution)/shard_map/ppermute | solution.py:95
  92.5 28.2 %collective-permute-done.4 = bf16[512,2048]{1,0:T(8,128)(2,1)S(1)} collective-permute-done((bf16[512,2048]{1,0:T(8,128)(2,1)S(1)}, bf16[512,2048]{1,0:T(8,128)(2,1)S(1)}, u32[]{:S(2)}, u32[]{:S(2)}) %collective-permute-start.4) | collective-permute-done | bytes 2097184 | tf_op jit(solution)/shard_map/ppermute | solution.py:95
  122.0 28.2 %collective-permute-done.5 = bf16[512,2048]{1,0:T(8,128)(2,1)S(1)} collective-permute-done((bf16[512,2048]{1,0:T(8,128)(2,1)S(1)}, bf16[512,2048]{1,0:T(8,128)(2,1)S(1)}, u32[]{:S(2)}, u32[]{:S(2)}) %collective-permute-start.5) | collective-permute-done | bytes 2097184 | tf_op jit(solution)/shard_map/ppermute | solution.py:95
  151.6 28.2 %collective-permute-done.6 = bf16[512,2048]{1,0:T(8,128)(2,1)S(1)} collective-permute-done((bf16[512,2048]{1,0:T(8,128)(2,1)S(1)}, bf16[512,2048]{1,0:T(8,128)(2,1)S(1)}, u32[]{:S(2)}, u32[]{:S(2)}) %collective-permute-start.6) | collective-permute-done | bytes 2097184 | tf_op jit(solution)/shard_map/ppermute | solution.py:95
  181.1 28.2 %collective-permute-done.7 = bf16[512,2048]{1,0:T(8,128)(2,1)S(1)} collective-permute-done((bf16[512,2048]{1,0:T(8,128)(2,1)S(1)}, bf16[512,2048]{1,0:T(8,128)(2,1)S(1)}, u32[]{:S(2)}, u32[]{:S(2)}) %collective-permute-start.7) | collective-permute-done | bytes 2097184 | tf_op jit(solution)/shard_map/ppermute | solution.py:95
  210.6 28.2 %collective-permute-done.8 = bf16[512,2048]{1,0:T(8,128)(2,1)S(1)} collective-permute-done((bf16[512,2048]{1,0:T(8,128)(2,1)S(1)}, bf16[512,2048]{1,0:T(8,128)(2,1)S(1)}, u32[]{:S(2)}, u32[]{:S(2)}) %collective-permute-start.8) | collective-permute-done | bytes 2097184 | tf_op jit(solution)/shard_map/ppermute | solution.py:95
  240.1 28.2 %collective-permute-done.9 = bf16[512,2048]{1,0:T(8,128)(2,1)S(1)} collective-permute-done((bf16[512,2048]{1,0:T(8,128)(2,1)S(1)}, bf16[512,2048]{1,0:T(8,128)(2,1)S(1)}, u32[]{:S(2)}, u32[]{:S(2)}) %collective-permute-start.9) | collective-permute-done | bytes 2097184 | tf_op jit(solution)/shard_map/ppermute | solution.py:95
  269.6 28.2 %collective-permute-done.10 = bf16[512,2048]{1,0:T(8,128)(2,1)S(1)} collective-permute-done((bf16[512,2048]{1,0:T(8,128)(2,1)S(1)}, bf16[512,2048]{1,0:T(8,128)(2,1)S(1)}, u32[]{:S(2)}, u32[]{:S(2)}) %collective-permute-start.10) | collective-permute-done | bytes 2097184 | tf_op jit(solution)/shard_map/ppermute | solution.py:95
  299.1 28.2 %collective-permute-done.11 = bf16[512,2048]{1,0:T(8,128)(2,1)S(1)} collective-permute-done((bf16[512,2048]{1,0:T(8,128)(2,1)S(1)}, bf16[512,2048]{1,0:T(8,128)(2,1)S(1)}, u32[]{:S(2)}, u32[]{:S(2)}) %collective-permute-start.11) | collective-permute-done | bytes 2097184 | tf_op jit(solution)/shard_map/ppermute | solution.py:95
  329.8 4.1 fusion.2
  333.9 21.6 %collective-permute-done.12 = bf16[512,2048]{1,0:T(8,128)(2,1)} collective-permute-done((bf16[512,2048]{1,0:T(8,128)(2,1)S(1)}, bf16[512,2048]{1,0:T(8,128)(2,1)}, u32[]{:S(2)}, u32[]{:S(2)}) %collective-permute-start.12) | collective-permute-done | bytes 2097184 | tf_op jit(solution)/shard_map/ppermute | solution.py:95
  355.5 4.7 fusion.4
  360.3 23.7 %collective-permute-done.13 = bf16[512,2048]{1,0:T(8,128)(2,1)} collective-permute-done((bf16[512,2048]{1,0:T(8,128)(2,1)}, bf16[512,2048]{1,0:T(8,128)(2,1)}, u32[]{:S(2)}, u32[]{:S(2)}) %collective-permute-start.13) | collective-permute-done | bytes 2097184 | tf_op jit(solution)/shard_map/ppermute | solution.py:95
  384.1 3.8 collective-permute-start
  389.5 4.9 gather_fusion
  396.2 16.3 %collective-permute-done.14 = bf16[512,2048]{1,0:T(8,128)(2,1)} collective-permute-done((bf16[512,2048]{1,0:T(8,128)(2,1)}, bf16[512,2048]{1,0:T(8,128)(2,1)}, u32[]{:S(2)}, u32[]{:S(2)}) %collective-permute-start.14) | collective-permute-done | bytes 2097184 | tf_op jit(solution)/shard_map/ppermute | solution.py:95
  413.1 2.6 copy.18
  421.0 19.9 %collective-permute-done.15 = bf16[512,2048]{1,0:T(8,128)(2,1)} collective-permute-done((bf16[512,2048]{1,0:T(8,128)(2,1)}, bf16[512,2048]{1,0:T(8,128)(2,1)}, u32[]{:S(2)}, u32[]{:S(2)}) %collective-permute-start.15) | collective-permute-done | bytes 2097184 | tf_op jit(solution)/shard_map/ppermute | solution.py:95
  440.9 3.2 constant_dynamic-update-slice_fusion.31
  444.1 3.3 constant_dynamic-update-slice_fusion.30
  447.4 3.3 constant_dynamic-update-slice_fusion.29
  450.8 3.3 constant_dynamic-update-slice_fusion.28
  473.2 3.1 constant_dynamic-update-slice_fusion.15
  476.3 3.2 constant_dynamic-update-slice_fusion.14
  479.5 3.1 constant_dynamic-update-slice_fusion.13
  482.7 3.2 constant_dynamic-update-slice_fusion.12
  504.8 15.7 %fusion.13 = f32[386,1536]{1,0:T(8,128)S(1)} fusion(bf16[16384,2048]{1,0:T(8,128)(2,1)} %constant_dynamic-update-slice_fusion, s32[]{:T(128)S(6)} %select_n.85, bf16[384,8192]{1,0:T(8,128)(2,1)} %copy-done.24, bf16[2,8192]{1,0:T(2,128)(2,1)S(1)} %collective-permute-done), kind=kOutput, calls=%fused_computation.21 | convolution fusion | flops 9727249408 | bytes 33861636 | tf_op jit(solution)/shard_map/dot_general | solution.py:102
  521.4 2.4 multiply_reduce_fusion.2
  525.1 3.8 collective-permute-start.16
  533.7 12.0 %fusion.8 = bf16[1,1,384,8192]{3,2,1,0:T(8,128)(2,1)} fusion(bf16[384,512]{1,0:T(8,128)(2,1)S(1)} %fusion.22, bf16[16384,2048]{1,0:T(8,128)(2,1)} %constant_dynamic-update-slice_fusion, s32[]{:T(128)S(6)} %select_n.85, s32[]{:T(128)S(6)} %add.126, bf16[1,1,384,8192]{3,2,1,0:T(8,128)(2,1)} %param.12, f32[8192]{0:T(1024)S(1)} %fusion.29, ...), kind=kOutput, calls=%fused_computation.15 | convolution fusion | flops 3236954112 | bytes 21397896 | tf_op jit(solution)/shard_map/dot_general | solution.py:125
  (140 shorter events, 70.3 us)
Async XLA Ops:
  0.0 387.9 %copy-start.26 = (f32[16,512]{1,0:T(8,128)S(1)}, f32[16,512]{1,0:T(8,128)}, u32[]{:S(2)}) copy-start(f32[16,512]{1,0:T(8,128)} %param.17) | copy-start | bytes 98308
  0.0 388.0 %copy-start.27 = (f32[16,512]{1,0:T(8,128)S(1)}, f32[16,512]{1,0:T(8,128)}, u32[]{:S(2)}) copy-start(f32[16,512]{1,0:T(8,128)} %param.18) | copy-start | bytes 98308
  2.9 29.2 %collective-permute-start.1 = (bf16[512,2048]{1,0:T(8,128)(2,1)S(1)}, bf16[512,2048]{1,0:T(8,128)(2,1)S(1)}, u32[]{:S(2)}, u32[]{:S(2)}) collective-permute-start(bf16[512,2048]{1,0:T(8,128)(2,1)S(1)} %pad_maximum_fusion), channel_id=1, source_target_pairs={{0,2},{2,4},{4,6},{6,8},{8,10},{10,12},{12,14},{14,16},{16,18},{18... | collective-permute-start | bytes 6291464 | tf_op jit(solution)/shard_map/ppermute | solution.py:95
  33.5 28.2 %collective-permute-start.2 = (bf16[512,2048]{1,0:T(8,128)(2,1)S(1)}, bf16[512,2048]{1,0:T(8,128)(2,1)S(1)}, u32[]{:S(2)}, u32[]{:S(2)}) collective-permute-start(bf16[512,2048]{1,0:T(8,128)(2,1)S(1)} %collective-permute-done.1), channel_id=1, source_target_pairs={{0,2},{2,4},{4,6},{6,8},{8,10},{10,12},{12,14},{14,16},{16,18},{18... | collective-permute-start | bytes 6291464 | tf_op jit(solution)/shard_map/ppermute | solution.py:95
  63.0 28.2 %collective-permute-start.3 = (bf16[512,2048]{1,0:T(8,128)(2,1)S(1)}, bf16[512,2048]{1,0:T(8,128)(2,1)S(1)}, u32[]{:S(2)}, u32[]{:S(2)}) collective-permute-start(bf16[512,2048]{1,0:T(8,128)(2,1)S(1)} %collective-permute-done.2), channel_id=1, source_target_pairs={{0,2},{2,4},{4,6},{6,8},{8,10},{10,12},{12,14},{14,16},{16,18},{18... | collective-permute-start | bytes 6291464 | tf_op jit(solution)/shard_map/ppermute | solution.py:95
  92.5 28.2 %collective-permute-start.4 = (bf16[512,2048]{1,0:T(8,128)(2,1)S(1)}, bf16[512,2048]{1,0:T(8,128)(2,1)S(1)}, u32[]{:S(2)}, u32[]{:S(2)}) collective-permute-start(bf16[512,2048]{1,0:T(8,128)(2,1)S(1)} %collective-permute-done.3), channel_id=1, source_target_pairs={{0,2},{2,4},{4,6},{6,8},{8,10},{10,12},{12,14},{14,16},{16,18},{18... | collective-permute-start | bytes 6291464 | tf_op jit(solution)/shard_map/ppermute | solution.py:95
  122.0 28.2 %collective-permute-start.5 = (bf16[512,2048]{1,0:T(8,128)(2,1)S(1)}, bf16[512,2048]{1,0:T(8,128)(2,1)S(1)}, u32[]{:S(2)}, u32[]{:S(2)}) collective-permute-start(bf16[512,2048]{1,0:T(8,128)(2,1)S(1)} %collective-permute-done.4), channel_id=1, source_target_pairs={{0,2},{2,4},{4,6},{6,8},{8,10},{10,12},{12,14},{14,16},{16,18},{18... | collective-permute-start | bytes 6291464 | tf_op jit(solution)/shard_map/ppermute | solution.py:95
  151.6 28.2 %collective-permute-start.6 = (bf16[512,2048]{1,0:T(8,128)(2,1)S(1)}, bf16[512,2048]{1,0:T(8,128)(2,1)S(1)}, u32[]{:S(2)}, u32[]{:S(2)}) collective-permute-start(bf16[512,2048]{1,0:T(8,128)(2,1)S(1)} %collective-permute-done.5), channel_id=1, source_target_pairs={{0,2},{2,4},{4,6},{6,8},{8,10},{10,12},{12,14},{14,16},{16,18},{18... | collective-permute-start | bytes 6291464 | tf_op jit(solution)/shard_map/ppermute | solution.py:95
  181.1 28.2 %collective-permute-start.7 = (bf16[512,2048]{1,0:T(8,128)(2,1)S(1)}, bf16[512,2048]{1,0:T(8,128)(2,1)S(1)}, u32[]{:S(2)}, u32[]{:S(2)}) collective-permute-start(bf16[512,2048]{1,0:T(8,128)(2,1)S(1)} %collective-permute-done.6), channel_id=1, source_target_pairs={{0,2},{2,4},{4,6},{6,8},{8,10},{10,12},{12,14},{14,16},{16,18},{18... | collective-permute-start | bytes 6291464 | tf_op jit(solution)/shard_map/ppermute | solution.py:95
  210.6 28.2 %collective-permute-start.8 = (bf16[512,2048]{1,0:T(8,128)(2,1)S(1)}, bf16[512,2048]{1,0:T(8,128)(2,1)S(1)}, u32[]{:S(2)}, u32[]{:S(2)}) collective-permute-start(bf16[512,2048]{1,0:T(8,128)(2,1)S(1)} %collective-permute-done.7), channel_id=1, source_target_pairs={{0,2},{2,4},{4,6},{6,8},{8,10},{10,12},{12,14},{14,16},{16,18},{18... | collective-permute-start | bytes 6291464 | tf_op jit(solution)/shard_map/ppermute | solution.py:95
  240.1 28.2 %collective-permute-start.9 = (bf16[512,2048]{1,0:T(8,128)(2,1)S(1)}, bf16[512,2048]{1,0:T(8,128)(2,1)S(1)}, u32[]{:S(2)}, u32[]{:S(2)}) collective-permute-start(bf16[512,2048]{1,0:T(8,128)(2,1)S(1)} %collective-permute-done.8), channel_id=1, source_target_pairs={{0,2},{2,4},{4,6},{6,8},{8,10},{10,12},{12,14},{14,16},{16,18},{18... | collective-permute-start | bytes 6291464 | tf_op jit(solution)/shard_map/ppermute | solution.py:95
  269.6 28.2 %collective-permute-start.10 = (bf16[512,2048]{1,0:T(8,128)(2,1)S(1)}, bf16[512,2048]{1,0:T(8,128)(2,1)S(1)}, u32[]{:S(2)}, u32[]{:S(2)}) collective-permute-start(bf16[512,2048]{1,0:T(8,128)(2,1)S(1)} %collective-permute-done.9), channel_id=1, source_target_pairs={{0,2},{2,4},{4,6},{6,8},{8,10},{10,12},{12,14},{14,16},{16,18},{18... | collective-permute-start | bytes 6291464 | tf_op jit(solution)/shard_map/ppermute | solution.py:95
  299.1 28.2 %collective-permute-start.11 = (bf16[512,2048]{1,0:T(8,128)(2,1)S(1)}, bf16[512,2048]{1,0:T(8,128)(2,1)S(1)}, u32[]{:S(2)}, u32[]{:S(2)}) collective-permute-start(bf16[512,2048]{1,0:T(8,128)(2,1)S(1)} %collective-permute-done.10), channel_id=1, source_target_pairs={{0,2},{2,4},{4,6},{6,8},{8,10},{10,12},{12,14},{14,16},{16,18},{18... | collective-permute-start | bytes 6291464 | tf_op jit(solution)/shard_map/ppermute | solution.py:95
  327.3 60.8 %copy-start.22 = (bf16[512,2048]{1,0:T(8,128)(2,1)}, bf16[512,2048]{1,0:T(8,128)(2,1)S(1)}, u32[]{:S(2)}) copy-start(bf16[512,2048]{1,0:T(8,128)(2,1)S(1)} %collective-permute-done.11) | copy-start | bytes 6291460
  327.3 28.3 %collective-permute-start.12 = (bf16[512,2048]{1,0:T(8,128)(2,1)S(1)}, bf16[512,2048]{1,0:T(8,128)(2,1)}, u32[]{:S(2)}, u32[]{:S(2)}) collective-permute-start(bf16[512,2048]{1,0:T(8,128)(2,1)S(1)} %collective-permute-done.11), channel_id=1, source_target_pairs={{0,2},{2,4},{4,6},{6,8},{8,10},{10,12},{12,14},{14,16},{16,18},{18... | collective-permute-start | bytes 6291464 | tf_op jit(solution)/shard_map/ppermute | solution.py:95
  355.5 28.5 %collective-permute-start.13 = (bf16[512,2048]{1,0:T(8,128)(2,1)}, bf16[512,2048]{1,0:T(8,128)(2,1)}, u32[]{:S(2)}, u32[]{:S(2)}) collective-permute-start(bf16[512,2048]{1,0:T(8,128)(2,1)} %collective-permute-done.12), channel_id=1, source_target_pairs={{0,2},{2,4},{4,6},{6,8},{8,10},{10,12},{12,14},{14,16},{16,18},{18... | collective-permute-start | bytes 6291464 | tf_op jit(solution)/shard_map/ppermute | solution.py:95
  360.3 23.7 %copy-start.24 = (bf16[384,8192]{1,0:T(8,128)(2,1)}, bf16[384,8192]{1,0:T(8,128)(2,1)S(1)}, u32[]{:S(2)}) copy-start(bf16[384,8192]{1,0:T(8,128)(2,1)S(1)} %fusion.4) | copy-start | bytes 18874372
  360.3 52.2 %copy-start.30 = (s32[1,2]{1,0:T(1,128)S(1)}, s32[1,2]{1,0:T(1,128)}, u32[]{:S(2)}) copy-start(s32[1,2]{1,0:T(1,128)} %param.13) | copy-start | bytes 28
  384.0 28.5 %collective-permute-start.14 = (bf16[512,2048]{1,0:T(8,128)(2,1)}, bf16[512,2048]{1,0:T(8,128)(2,1)}, u32[]{:S(2)}, u32[]{:S(2)}) collective-permute-start(bf16[512,2048]{1,0:T(8,128)(2,1)} %collective-permute-done.13), channel_id=1, source_target_pairs={{0,2},{2,4},{4,6},{6,8},{8,10},{10,12},{12,14},{14,16},{16,18},{18... | collective-permute-start | bytes 6291464 | tf_op jit(solution)/shard_map/ppermute | solution.py:95
  384.1 120.7 %collective-permute-start = (bf16[2,8192]{1,0:T(2,128)(2,1)S(1)}, bf16[2,8192]{1,0:T(2,128)(2,1)S(1)}, u32[]{:S(2)}, u32[]{:S(2)}) collective-permute-start(bf16[2,8192]{1,0:T(2,128)(2,1)S(1)} %constant_dynamic-slice_fusion.1), channel_id=1, source_target_pairs={{0,1},{2,3},{4,5},{6,7},{8,9},{10,11},{12,13},{14,15},{16,17},{18,... | collective-permute-start | bytes 98312 | tf_op jit(solution)/shard_map/ppermute | solution.py:13
  389.5 29.3 %copy-start.28 = (f32[3,1536]{1,0:T(4,128)S(1)}, f32[3,1536]{1,0:T(4,128)}, u32[]{:S(2)}) copy-start(f32[3,1536]{1,0:T(4,128)} %param.16) | copy-start | bytes 55300
  412.5 28.5 %collective-permute-start.15 = (bf16[512,2048]{1,0:T(8,128)(2,1)}, bf16[512,2048]{1,0:T(8,128)(2,1)}, u32[]{:S(2)}, u32[]{:S(2)}) collective-permute-start(bf16[512,2048]{1,0:T(8,128)(2,1)} %collective-permute-done.14), channel_id=1, source_target_pairs={{0,2},{2,4},{4,6},{6,8},{8,10},{10,12},{12,14},{14,16},{16,18},{18... | collective-permute-start | bytes 6291464 | tf_op jit(solution)/shard_map/ppermute | solution.py:95
  415.7 40.0 %copy-start.21 = (bf16[512,2048]{1,0:T(8,128)(2,1)S(1)}, bf16[512,2048]{1,0:T(8,128)(2,1)}, u32[]{:S(2)}) copy-start(bf16[512,2048]{1,0:T(8,128)(2,1)} %copy-done.20) | copy-start | bytes 6291460
  418.0 36.2 %copy-start.23 = (bf16[512,2048]{1,0:T(8,128)(2,1)S(1)}, bf16[512,2048]{1,0:T(8,128)(2,1)}, u32[]{:S(2)}) copy-start(bf16[512,2048]{1,0:T(8,128)(2,1)} %copy-done.22) | copy-start | bytes 6291460
  421.0 36.2 %copy-start.19 = (bf16[512,2048]{1,0:T(8,128)(2,1)S(1)}, bf16[512,2048]{1,0:T(8,128)(2,1)}, u32[]{:S(2)}) copy-start(bf16[512,2048]{1,0:T(8,128)(2,1)} %copy-done.18) | copy-start | bytes 6291460
  444.1 14.7 %copy-start.17 = (bf16[512,2048]{1,0:T(8,128)(2,1)S(1)}, bf16[512,2048]{1,0:T(8,128)(2,1)}, u32[]{:S(2)}) copy-start(bf16[512,2048]{1,0:T(8,128)(2,1)} %copy-done.16) | copy-start | bytes 6291460
  447.4 13.0 %copy-start.15 = (bf16[512,2048]{1,0:T(8,128)(2,1)S(1)}, bf16[512,2048]{1,0:T(8,128)(2,1)}, u32[]{:S(2)}) copy-start(bf16[512,2048]{1,0:T(8,128)(2,1)} %copy-done.14) | copy-start | bytes 6291460
  450.8 11.2 %copy-start.13 = (bf16[512,2048]{1,0:T(8,128)(2,1)S(1)}, bf16[512,2048]{1,0:T(8,128)(2,1)}, u32[]{:S(2)}) copy-start(bf16[512,2048]{1,0:T(8,128)(2,1)} %copy-done.12) | copy-start | bytes 6291460
  462.0 9.6 %copy-start = (bf16[512,1536]{1,0:T(8,128)(2,1)S(1)}, bf16[512,1536]{1,0:T(8,128)(2,1)}, u32[]{:S(2)}) copy-start(bf16[512,1536]{1,0:T(8,128)(2,1)} %param.15) | copy-start | bytes 4718596
  520.5 11.7 %copy-start.25 = (f32[16,32,512]{2,1,0:T(8,128)S(1)}, f32[16,32,512]{2,1,0:T(8,128)}, u32[]{:S(2)}) copy-start(f32[16,32,512]{2,1,0:T(8,128)} %exponential_multiply_fusion) | copy-start | bytes 3145732
  520.5 12.9 %copy-start.29 = (f32[512]{0:T(512)S(1)}, f32[512]{0:T(512)}, u32[]{:S(2)}) copy-start(f32[512]{0:T(512)} %param.19) | copy-start | bytes 6148
  525.1 6.3 %collective-permute-start.16 = (f32[16,512]{1,0:T(8,128)S(1)}, f32[16,512]{1,0:T(8,128)S(1)}, u32[]{:S(2)}, u32[]{:S(2)}) collective-permute-start(f32[16,512]{1,0:T(8,128)S(1)} %fusion.27), channel_id=1, source_target_pairs={{0,1},{2,3},{4,5},{6,7},{8,9},{10,11},{12,13},{14,15},{16,17},{18,... | collective-permute-start | bytes 98312 | tf_op jit(solution)/shard_map/ppermute | solution.py:13
  (16 other events, 69.5 us)
